TPU v7x, 32 devices: a whole 2x2x4 slice. The times are simulated.
32 devices in a mesh: groups: 2 (over y), tensor: 8 (over z, x), dp: 2 (over core).
Axes of the slice: x: 2, y: 2, z: 4, core: 2. Of those that a mesh axis runs over, the one named last changes fastest.
Arguments:
- hidden: bfloat16 [2400, 8192], P(('groups', 'dp'), 'tensor'), parts along dimension 0, may hold values from -6 to 6
- norm_gain: float32 [8192], replicated, may hold values from 0.1 to 1.9
- query_weight: bfloat16 [8192, 8192], P('dp', 'tensor'), may hold values from -0.09375 to 0.09375
- query_keep: int32 [128, 128], P('dp', 'tensor'), may hold values 0 or 1
- kv_weight: bfloat16 [2048, 8192], P('tensor', 'dp'), may hold values from -0.0625 to 0.0625
- out_weight: bfloat16 [8192, 8192], P('tensor', 'dp'), may hold values from -0.5 to 0.5
- out_keep: int32 [128, 128], P('tensor', 'dp'), may hold values 0 or 1
- pair_lengths: int32 [4, 4], P(('groups', 'dp')), parts along dimension 0, may hold values from 1 to 300, 600 in all within a row
- premise_lengths: int32 [4, 4], P(('groups', 'dp')), parts along dimension 0, may hold values from 1 to 299
Outputs:
- attn_out: bfloat16 [2400, 8192], P(('groups', 'dp'), 'tensor'), parts along dimension 0
There are 2 independent parts, one for each index of `groups`. A program takes and returns all parts, laid end to end along the dimension named above; an argument that names none is the same for every part. Nothing has to cross between parts.
Inputs may be any that keep to these rules, and one draw needn't show every extreme that they name: `pair_lengths`: each row lists the 4 pair lengths of one batch in order; they sum to 600.
All inputs are finite; a program needn't handle non-finite values. No bound on the sum of `query_keep` or of `out_keep` on one device may be relied on, other than what follows from the above.
Results may differ from a plain program's by a relative error of at most 0.01.
Values may be sent and summed in bfloat16 or wider, within the bound.
No kernel may reach another device: no remote copies, remote signals or barrier semaphores. Data moves between devices by JAX's collectives and lax.ppermute only.
A program may use at most 192 MiB of HBM per device.

v0:
```python
import jax
import jax.numpy as jnp
from jax import lax
from jax.sharding import PartitionSpec as P

HEADS = 64
KVH = 8
HD = 128


def rotate_pairs(values, positions):
    half_width = values.shape[-1] // 2
    inverse = 500000.0 ** (-(jnp.arange(half_width, dtype=jnp.float32) * 2.0 / values.shape[-1]))
    angles = positions[:, None] * inverse[None, :]
    cosine = jnp.cos(angles)[:, None, :]
    sine_part = jnp.sin(angles)[:, None, :]
    first_half = values[..., :half_width]
    second_half = values[..., half_width:]
    return jnp.concatenate(
        [
            first_half * cosine - second_half * sine_part,
            second_half * cosine + first_half * sine_part,
        ],
        axis=-1,
    )


def pair_layout(lengths, premise, count):
    pair_ends = jnp.cumsum(lengths)
    pair_starts = pair_ends - lengths
    position = jnp.arange(count, dtype=jnp.int32)
    pair_index = jnp.sum((position[:, None] >= pair_ends[None, :]).astype(jnp.int32), axis=1)
    one_hot = (
        pair_index[:, None] == jnp.arange(lengths.shape[0], dtype=jnp.int32)[None, :]
    ).astype(jnp.int32)
    offset = position - jnp.sum(one_hot * pair_starts[None, :], axis=1)
    premise_used = jnp.minimum(premise, lengths - 1)
    in_premise = offset < jnp.sum(one_hot * premise_used[None, :], axis=1)
    allowed = (pair_index[:, None] == pair_index[None, :]) & (
        in_premise[None, :] | jnp.logical_not(in_premise)[:, None]
    )
    return (offset.astype(jnp.float32), allowed)


def prune(weight, keep):
    blocks = weight.reshape(
        keep.shape[0],
        weight.shape[0] // keep.shape[0],
        keep.shape[1],
        weight.shape[1] // keep.shape[1],
    )
    blocks = blocks * keep.astype(weight.dtype)[:, None, :, None]
    return blocks.reshape(weight.shape)


def on_device(
    hidden,
    norm_gain,
    query_weight,
    query_keep,
    kv_weight,
    out_weight,
    out_keep,
    pair_lengths,
    premise_lengths,
):
    tensor_rank = lax.axis_index("tensor")
    total_rows = hidden.shape[0]
    head_local = query_weight.shape[1] // HD
    query_pruned = prune(query_weight, query_keep)
    out_pruned = prune(out_weight, out_keep)
    query_full = lax.all_gather(query_pruned, "dp", axis=0, tiled=True)
    kv_full, out_full = (
        lax.all_gather(kv_weight, "dp", axis=1, tiled=True),
        lax.all_gather(out_pruned, "dp", axis=1, tiled=True),
    )
    whole = lax.all_gather(hidden, "tensor", axis=1, tiled=True)
    rows_float = whole.astype(jnp.float32)
    mean_square = jnp.mean(rows_float * rows_float, axis=-1, keepdims=True)
    normed = (rows_float * lax.rsqrt(mean_square + 1e-05) * norm_gain).astype(jnp.bfloat16)
    queries_raw = jnp.dot(normed, query_full, preferred_element_type=jnp.float32)
    kv_piece = lax.dot_general(
        normed, kv_full, (((1,), (1,)), ((), ())), preferred_element_type=jnp.float32
    ).astype(jnp.bfloat16)
    kv_whole = lax.all_gather(kv_piece, "tensor", axis=1, tiled=True)
    offsets, allowed = pair_layout(pair_lengths[0], premise_lengths[0], total_rows)
    queries = rotate_pairs(queries_raw.reshape(total_rows, head_local, HD), offsets).astype(
        jnp.bfloat16
    )
    keys_all = rotate_pairs(
        kv_whole[:, : KVH * HD].reshape(total_rows, KVH, HD).astype(jnp.float32), offsets
    ).astype(jnp.bfloat16)
    values_all = kv_whole[:, KVH * HD :].reshape(total_rows, KVH, HD)
    chosen = (tensor_rank * head_local + jnp.arange(head_local, dtype=jnp.int32)) // (HEADS // KVH)
    keys_used = jnp.take(keys_all, chosen, axis=1)
    values_used = jnp.take(values_all, chosen, axis=1)
    count_blocks = total_rows // total_rows
    scale = HD ** (-0.5)

    def attend(operands):
        query_block, allowed_block = operands
        scores = (
            jnp.einsum("qhd,khd->hqk", query_block, keys_used, preferred_element_type=jnp.float32)
            * scale
        )
        weighted = jnp.where(allowed_block[None, :, :], jnp.exp(scores), 0.0)
        probs = (weighted / jnp.sum(weighted, axis=-1, keepdims=True)).astype(jnp.bfloat16)
        return jnp.einsum(
            "hqk,khd->qhd", probs, values_used, preferred_element_type=jnp.float32
        ).astype(jnp.bfloat16)

    context = lax.map(
        attend,
        (
            queries.reshape(count_blocks, total_rows, head_local, HD),
            allowed.reshape(count_blocks, total_rows, total_rows),
        ),
    )
    context = context.reshape(total_rows, head_local * HD)
    terms = jnp.dot(context, out_full, preferred_element_type=jnp.float32)
    mixed = lax.psum_scatter(terms, "tensor", scatter_dimension=1, tiled=True)
    return mixed.astype(jnp.bfloat16)


def solution(mesh):
    placed = (
        P(("groups", "dp"), "tensor"),
        P(),
        P("dp", "tensor"),
        P("dp", "tensor"),
        P("tensor", "dp"),
        P("tensor", "dp"),
        P("tensor", "dp"),
        P(("groups", "dp"), None),
        P(("groups", "dp"), None),
    )
    return jax.shard_map(
        on_device,
        mesh=mesh,
        in_specs=placed,
        out_specs=P(("groups", "dp"), "tensor"),
        check_vma=False,
    )
```

profile of v0, /device:TPU:0, one launch (start us, length us, event | category | flops | bytes accessed | tf_op | source)
XLA Modules:
  0.0 643.1 jit_solution(441192260038344043)
XLA Ops:
  8.2 6.2 mul.162
  14.4 22.8 %mul.163 = bf16[4096,1024]{1,0:T(8,128)(2,1)} reshape(bf16[64,64,16,64]{3,2,1,0:T(8,128)(2,1)} %mul.162) | data formatting | bytes 16777216 | tf_op jit(solution)/shard_map/mul | solution.py:52
  37.2 10.7 %mul.164 = bf16[4096,1024]{1,0:T(8,128)(2,1)} multiply(bf16[4096,1024]{1,0:T(8,128)(2,1)} %param.13, bf16[4096,1024]{1,0:T(8,128)(2,1)} %mul.163) | non-fusion elementwise | flops 4194304 | bytes 25165824 | tf_op jit(solution)/shard_map/mul | solution.py:52
  48.0 106.5 %all-gather.6.cloned.1.call-done = bf16[600,8192]{1,0:T(8,128)(2,1)} async-done(((bf16[600,1024]{1,0:T(8,128)(2,1)}), bf16[600,8192]{1,0:T(8,128)(2,1)}) %all-gather.6.cloned.1.call-update) | async-done | bytes 9830416 | tf_op jit(solution)/shard_map/all_gather | solution.py:77
  154.5 5.8 fusion
  160.3 7.7 %all-gather.8.cloned.1.call-done = bf16[256,8192]{1,0:T(8,128)(2,1)} async-done(((bf16[256,4096]{1,0:T(8,128)(2,1)}), bf16[256,8192]{1,0:T(8,128)(2,1)}) %all-gather.8.cloned.1.call-update) | async-done | bytes 4194320 | tf_op jit(solution)/shard_map/all_gather | solution.py:74
  168.0 8.6 %fusion.27 = bf16[600,256]{1,0:T(8,128)(2,1)} fusion(bf16[256,8192]{1,0:T(8,128)(2,1)} %all-gather.8.cloned.1.call-done, bf16[600,8192]{1,0:T(8,128)(2,1)} %all-gather.6.cloned.1.call-done, f32[8192]{0:T(1024)S(1)} %copy-done.5, f32[600]{0:T(1024)S(1)} %add_rsqrt_fusion), kind=kOutput, calls=%fused_computation.38 | convolution fusion | flops 2536396800 | bytes 14367072 | tf_op jit(solution)/shard_map/dot_general | solution.py:82
  176.7 10.6 %mul.179 = bf16[16,64,64,64]{3,2,1,0:T(8,128)(2,1)} broadcast(bf16[16,64]{1,0:T(8,128)(2,1)S(1)} %convert_element_type.59), dimensions={0,2} | broadcast | bytes 8390656 | tf_op jit(solution)/shard_map/mul | solution.py:52
  187.3 23.1 %mul.180 = bf16[1024,4096]{1,0:T(8,128)(2,1)} reshape(bf16[16,64,64,64]{3,2,1,0:T(8,128)(2,1)} %mul.179) | data formatting | bytes 16777216 | tf_op jit(solution)/shard_map/mul | solution.py:52
  210.4 10.3 %mul.181 = bf16[1024,4096]{1,0:T(8,128)(2,1)} multiply(bf16[1024,4096]{1,0:T(8,128)(2,1)} %param.16, bf16[1024,4096]{1,0:T(8,128)(2,1)} %mul.180) | non-fusion elementwise | flops 4194304 | bytes 25165824 | tf_op jit(solution)/shard_map/mul | solution.py:52
  222.2 1.1 multiply_cosine_fusion
  223.4 15.6 %fusion.9 = f32[75,8,8,128]{3,1,2,0:T(8,128)S(1)} fusion(bf16[8192,1024]{1,0:T(8,128)(2,1)} %all-gather.12.cloned.1.call-done, bf16[600,8192]{1,0:T(8,128)(2,1)} %all-gather.6.cloned.1.call-done, f32[8192]{0:T(1024)S(1)} %copy-done.5, f32[600]{0:T(1024)S(1)} %add_rsqrt_fusion), kind=kOutput, calls=%fused_computation.18 | convolution fusion | flops 10085990400 | bytes 29100384 | tf_op jit(solution)/shard_map/dot_general | solution.py:81
  239.6 19.9 %all-gather.10.cloned.1.call-done = bf16[600,2048]{1,0:T(8,128)(2,1)} async-done(((bf16[600,256]{1,0:T(8,128)(2,1)}), bf16[600,2048]{1,0:T(8,128)(2,1)}) %all-gather.10.cloned.1.call-update) | async-done | bytes 2457616 | tf_op jit(solution)/shard_map/all_gather | solution.py:85
  259.4 2.1 slice_bitcast_fusion
  262.1 1.3 copy.54
  263.4 1.9 fusion.42
  265.3 2.9 subtract_convert_fusion
  268.8 1.7 gather_fusion.1
  271.3 6.8 %fusion.3 = (f32[8,600]{1,0:T(8,128)S(1)}, f32[8,600,600]{1,2,0:T(8,128)S(1)}) fusion(pred[600,600]{0,1:T(8,128)(4,1)S(1)} %or_and_fusion, bf16[8,600,128]{2,1,0:T(8,128)(2,1)} %gather_fusion.1, pred[8]{0:T(512)(128)(4,1)S(1)} %compare_and_fusion, bf16[600,8,64]{2,0,1:T(8,128)(2,1)} %get-tuple-element.38, bf16[600,8,64]{2,0,1:T(8,128)(2,1)} %get-tuple-element.39), kind=kOutput, calls=%fused_computation.9 | convolution fusion | flops 748987200 | bytes 14356808 | tf_op jit(solution)/shard_map/while/body/eval_jaxpr/qhd,khd->hqk/dot_general | solution.py:103
  278.1 4.4 fusion.13
  282.6 6.6 %all-gather.14.cloned.1.call-done = bf16[1024,8192]{1,0:T(8,128)(2,1)} async-done(((bf16[1024,4096]{1,0:T(8,128)(2,1)}), bf16[1024,8192]{1,0:T(8,128)(2,1)}) %all-gather.14.cloned.1.call-update) | async-done | bytes 16777232 | tf_op jit(solution)/shard_map/all_gather | solution.py:75
  289.2 17.6 %fusion.14 = f32[600,8192]{1,0:T(8,128)} fusion(bf16[1024,8192]{1,0:T(8,128)(2,1)} %all-gather.14.cloned.1.call-done, bf16[8,75,8,128]{3,2,1,0:T(8,128)(2,1)S(1)} %fusion.13), kind=kOutput, calls=%fused_computation.22 | convolution fusion | flops 10066329600 | bytes 37666816 | tf_op jit(solution)/shard_map/dot_general | solution.py:120
  306.8 326.6 %reduce-scatter.2.cloned.1.call-done = f32[600,1024]{1,0:T(8,128)} async-done(((f32[600,8192]{1,0:T(8,128)}), f32[600,1024]{1,0:T(8,128)}) %reduce-scatter.2.cloned.1.call-update) | async-done | bytes 2457616 | tf_op jit(solution)/shard_map/reduce_scatter | solution.py:121
  633.4 2.9 convert_element_type.60
  (44 shorter events, 5.8 us)
Async XLA Ops:
  6.5 1.5 copy-start.1
  6.5 148.0 %all-gather.6.cloned.1.call-start = ((), (), s32[]{:S(2)}) async-start(), calls=%async_computation.1 | async-start | bytes 11059200 | tf_op jit(solution)/shard_map/all_gather | solution.py:77
  7.3 160.7 %all-gather.8.cloned.1.call-start = ((), (), s32[]{:S(2)}) async-start(), calls=%async_computation.2 | async-start | bytes 6291456 | tf_op jit(solution)/shard_map/all_gather | solution.py:74
  8.0 215.4 %all-gather.12.cloned.1.call-start = ((), (), s32[]{:S(2)}) async-start(), calls=%async_computation.4 | async-start | bytes 25165824 | tf_op jit(solution)/shard_map/all_gather | solution.py:72
  47.9 120.1 %copy-start.5 = (f32[8192]{0:T(1024)S(1)}, f32[8192]{0:T(1024)}, u32[]{:S(2)}) copy-start(f32[8192]{0:T(1024)} %param.12) | copy-start | bytes 98308
  47.9 211.5 %all-gather.10.cloned.1.call-start = ((), (), s32[]{:S(2)}) async-start(), calls=%async_computation.3 | async-start | bytes 2764800 | tf_op jit(solution)/shard_map/all_gather | solution.py:85
  160.3 16.4 %copy-start.2 = (s32[16,64]{1,0:T(8,128)S(1)}, s32[16,64]{1,0:T(8,128)}, u32[]{:S(2)}) copy-start(s32[16,64]{1,0:T(8,128)} %param.17) | copy-start | bytes 12292
  176.6 112.5 %all-gather.14.cloned.1.call-start = ((), (), s32[]{:S(2)}) async-start(), calls=%async_computation.5 | async-start | bytes 25165824 | tf_op jit(solution)/shard_map/all_gather | solution.py:75
  220.7 0.7 copy-start.3
  220.7 1.0 copy-start.4
  220.8 412.6 %reduce-scatter.2.cloned.1.call-start = ((), (), s32[]{:S(2)}) async-start(), calls=%async_computation.6 | async-start | bytes 22118400 | tf_op jit(solution)/shard_map/reduce_scatter | solution.py:121
  268.1 2.4 copy-start
Sparse Core Ops, SparseCore 0:
  9.5 144.9 all-gather.5
  156.0 11.8 all-gather.7
  169.5 31.1 all-gather.11
  202.6 56.7 all-gather.9
  260.8 28.2 all-gather.13
  306.9 326.4 reduce-scatter.1
where the time goes:
time: 644 us; the launch traced here: 643 us
  waiting for transfers between devices  469 us (73%)
  local copies, waits for them, and re-layouts  70 us (11%)
  matrix products  53 us (8%)
  other arithmetic  37.3 us (6%)
  between operations  13.7 us (2%)
    reduce_scatter x1, waiting for transfers between devices, on_device(): mixed = lax.psum_scatter(terms, 'tensor', scatter_dimension=1, tiled=True)  327 us
    all_gather x1, waiting for transfers between devices, on_device(): whole = lax.all_gather(hidden, 'tensor', axis=1, tiled=True)  107 us
    mul x4, local copies, waits for them, and re-layouts, prune(): blocks = blocks * keep.astype(weight.dtype)[:, None, :, None]  62.7 us
    mul x2, other arithmetic, prune(): blocks = blocks * keep.astype(weight.dtype)[:, None, :, None]  21 us
    all_gather x1, waiting for transfers between devices, on_device(): kv_whole = lax.all_gather(kv_piece, 'tensor', axis=1, tiled=True)  19.9 us
    dot_general x1, matrix products, on_device(): terms = jnp.dot(context, out_full, preferred_element_type=jnp.float32)  17.6 us
    dot_general x1, matrix products, on_device(): jnp.dot(normed, query_full, preferred_element_type=jnp.float32)  15.6 us
  transfers between devices with their start and end apart: 6, of which 5 were waited for; matrix products, arithmetic and copies ran while one was open for 22% of the time, Pallas kernels for 0%

commit v1 on v0

--- a/solution.py
+++ b/solution.py
@@ -74,7 +74,15 @@
         lax.all_gather(kv_weight, "dp", axis=1, tiled=True),
         lax.all_gather(out_pruned, "dp", axis=1, tiled=True),
     )
-    whole = lax.all_gather(hidden, "tensor", axis=1, tiled=True)
+    ways, here = (lax.axis_size("tensor"), lax.axis_index("tensor"))
+    grown, reach = (hidden, 1)
+    while reach < ways:
+        theirs = lax.ppermute(grown, "tensor", [(d, d ^ reach) for d in range(ways)])
+        mine_first = jnp.concatenate([grown, theirs], axis=1)
+        theirs_first = jnp.concatenate([theirs, grown], axis=1)
+        grown = jnp.where(here & reach == 0, mine_first, theirs_first)
+        reach = 2 * reach
+    whole = grown
     rows_float = whole.astype(jnp.float32)
     mean_square = jnp.mean(rows_float * rows_float, axis=-1, keepdims=True)
     normed = (rows_float * lax.rsqrt(mean_square + 1e-05) * norm_gain).astype(jnp.bfloat16)

time: 644 us -> 827 us (1.28)
  waiting for transfers between devices: 469 us -> 616 us
  other arithmetic: 37.3 us -> 56.9 us
  matrix products: 53 us -> 63.8 us
    ppermute x0 -> x3, waiting for transfers between devices: none -> 290 us  [on_device(): lax.ppermute(grown, 'tensor', [(d, d ^ reach) for d in range(ways)])]
    all_gather x1 -> x0, waiting for transfers between devices: 107 us -> none  [on_device(): whole = lax.all_gather(hidden, 'tensor', axis=1, tiled=True)]
    all_gather x1, waiting for transfers between devices: 19.9 us -> 0.02 us  [on_device(): kv_whole = lax.all_gather(kv_piece, 'tensor', axis=1, tiled=True)]
    select_n x0 -> x2, other arithmetic: none -> 10.2 us  [on_device(): grown = jnp.where(here & reach == 0, mine_first, theirs_first)]
    dot_general x1, matrix products: 15.6 us -> 24.5 us  [on_device(): jnp.dot(normed, query_full, preferred_element_type=jnp.float32)]
  transfers between devices with their start and end apart: 6 -> 8, of which waited for: 5 -> 4; matrix products, arithmetic and copies ran while one was open for 22% -> 18% of each run, Pallas kernels for 0% -> 0%
where the time goes in v1:
time: 827 us; the launch traced here: 826 us
  waiting for transfers between devices  616 us (74%)
  local copies, waits for them, and re-layouts  67.4 us (8%)
  matrix products  63.8 us (8%)
  other arithmetic  56.9 us (7%)
  between operations  13.4 us (2%)
    reduce_scatter x1, waiting for transfers between devices, on_device(): mixed = lax.psum_scatter(terms, 'tensor', scatter_dimension=1, tiled=True)  326 us
    ppermute x3, waiting for transfers between devices, on_device(): lax.ppermute(grown, 'tensor', [(d, d ^ reach) for d in range(ways)])  290 us
    mul x4, local copies, waits for them, and re-layouts, prune(): blocks = blocks * keep.astype(weight.dtype)[:, None, :, None]  58.3 us
    dot_general x1, matrix products, on_device(): jnp.dot(normed, query_full, preferred_element_type=jnp.float32)  24.5 us
    mul x2, other arithmetic, prune(): blocks = blocks * keep.astype(weight.dtype)[:, None, :, None]  24.4 us
    dot_general x1, matrix products, on_device(): terms = jnp.dot(context, out_full, preferred_element_type=jnp.float32)  17.8 us
  transfers between devices with their start and end apart: 8, of which 4 were waited for; matrix products, arithmetic and copies ran while one was open for 18% of the time, Pallas kernels for 0%

profile of v1, /device:TPU:0, one launch (start us, length us, event | category | flops | bytes accessed | tf_op | source)
XLA Modules:
  0.0 825.6 jit_solution(17152097216322664762)
XLA Ops:
  6.5 3.0 collective-permute-start
  9.5 27.3 %collective-permute-done = bf16[600,1024]{1,0:T(8,128)(2,1)} collective-permute-done((bf16[600,1024]{1,0:T(8,128)(2,1)}, bf16[600,1024]{1,0:T(8,128)(2,1)}, u32[]{:S(2)}, u32[]{:S(2)}) %collective-permute-start) | collective-permute-done | bytes 1228832 | tf_op jit(solution)/shard_map/ppermute | solution.py:80
  36.8 3.5 maximum_select_fusion.2
  42.2 52.8 %collective-permute-done.1 = bf16[600,2048]{1,0:T(8,128)(2,1)} collective-permute-done((bf16[600,2048]{1,0:T(8,128)(2,1)S(1)}, bf16[600,2048]{1,0:T(8,128)(2,1)}, u32[]{:S(2)}, u32[]{:S(2)}) %collective-permute-start.1) | collective-permute-done | bytes 2457632 | tf_op jit(solution)/shard_map/ppermute | solution.py:80
  95.0 6.7 maximum_select_fusion.1
  101.7 2.6 collective-permute-start.2
  104.4 210.2 %collective-permute-done.2 = bf16[600,4096]{1,0:T(8,128)(2,1)} collective-permute-done((bf16[600,4096]{1,0:T(8,128)(2,1)}, bf16[600,4096]{1,0:T(8,128)(2,1)}, u32[]{:S(2)}, u32[]{:S(2)}) %collective-permute-start.2) | collective-permute-done | bytes 4915232 | tf_op jit(solution)/shard_map/ppermute | solution.py:80
  314.6 11.8 %fusion = f32[600]{0:T(1024)S(1)} fusion(bf16[600,4096]{1,0:T(8,128)(2,1)} %maximum_select_fusion.1, bf16[600,4096]{1,0:T(8,128)(2,1)} %collective-permute-done.2, pred[]{:T(512)S(6)} %eq.35), kind=kLoop, calls=%fused_computation.4 | loop fusion | flops 58981800 | bytes 9832801 | tf_op jit(solution)/shard_map/reduce_sum | solution.py:87
  326.5 11.6 %fusion.27 = bf16[600,256]{1,0:T(8,128)(2,1)} fusion(bf16[256,8192]{1,0:T(8,128)(2,1)} %all-gather.5.cloned.1.call-done, f32[8192]{0:T(1024)S(1)} %copy-done.5, f32[600]{0:T(1024)S(1)} %add_rsqrt_fusion, bf16[600,4096]{1,0:T(8,128)(2,1)} %collective-permute-done.2, bf16[600,4096]{1,0:T(8,128)(2,1)} %maximum_select_fusion.1, pred[]{:T(512)S(6)} %eq.35), kind=kOutput, calls=%fused_computation.41 | convolution fusion | flops 2580633600 | bytes 14367073 | tf_op jit(solution)/shard_map/dot_general | solution.py:90
  338.3 6.1 mul.162
  344.4 22.6 %mul.163 = bf16[4096,1024]{1,0:T(8,128)(2,1)} reshape(bf16[64,64,16,64]{3,2,1,0:T(8,128)(2,1)} %mul.162) | data formatting | bytes 16777216 | tf_op jit(solution)/shard_map/mul | solution.py:52
  366.9 10.8 %mul.164 = bf16[4096,1024]{1,0:T(8,128)(2,1)} multiply(bf16[4096,1024]{1,0:T(8,128)(2,1)} %param.13, bf16[4096,1024]{1,0:T(8,128)(2,1)} %mul.163) | non-fusion elementwise | flops 4194304 | bytes 25165824 | tf_op jit(solution)/shard_map/mul | solution.py:52
  378.4 6.4 mul.179
  384.8 23.2 %mul.180 = bf16[1024,4096]{1,0:T(8,128)(2,1)} reshape(bf16[16,64,64,64]{3,2,1,0:T(8,128)(2,1)} %mul.179) | data formatting | bytes 16777216 | tf_op jit(solution)/shard_map/mul | solution.py:52
  408.1 13.7 %mul.181 = bf16[1024,4096]{1,0:T(8,128)(2,1)} multiply(bf16[1024,4096]{1,0:T(8,128)(2,1)} %param.16, bf16[1024,4096]{1,0:T(8,128)(2,1)} %mul.180) | non-fusion elementwise | flops 4194304 | bytes 25165824 | tf_op jit(solution)/shard_map/mul | solution.py:52
  424.4 2.1 slice_bitcast_fusion
  428.3 3.0 gather_fusion
  431.3 24.5 %fusion.9 = f32[75,8,8,128]{3,1,2,0:T(8,128)S(1)} fusion(bf16[8192,1024]{1,0:T(8,128)(2,1)} %all-gather.9.cloned.1.call-done, f32[8192]{0:T(1024)S(1)} %copy-done.5, f32[600]{0:T(1024)S(1)} %add_rsqrt_fusion, bf16[600,4096]{1,0:T(8,128)(2,1)} %collective-permute-done.2, bf16[600,4096]{1,0:T(8,128)(2,1)} %maximum_select_fusion.1, pred[]{:T(512)S(6)} %eq.35), kind=kOutput, calls=%fused_computation.21 | convolution fusion | flops 10130227200 | bytes 29100384 | tf_op jit(solution)/shard_map/dot_general | solution.py:89
  458.2 2.9 subtract_convert_fusion
  462.5 5.5 fusion.3
  468.0 4.4 fusion.13
  472.5 17.8 %fusion.14 = f32[600,8192]{1,0:T(8,128)} fusion(bf16[1024,8192]{1,0:T(8,128)(2,1)} %all-gather.11.cloned.1.call-done, bf16[8,75,8,128]{3,2,1,0:T(8,128)(2,1)S(1)} %fusion.13), kind=kOutput, calls=%fused_computation.25 | convolution fusion | flops 10066329600 | bytes 37666816 | tf_op jit(solution)/shard_map/dot_general | solution.py:128
  490.4 325.8 %reduce-scatter.2.cloned.1.call-done = f32[600,1024]{1,0:T(8,128)} async-done(((f32[600,8192]{1,0:T(8,128)}), f32[600,1024]{1,0:T(8,128)}) %reduce-scatter.2.cloned.1.call-update) | async-done | bytes 2457616 | tf_op jit(solution)/shard_map/reduce_scatter | solution.py:129
  816.1 2.9 convert_element_type.60
  (49 shorter events, 11.1 us)
Async XLA Ops:
  6.5 319.9 %all-gather.5.cloned.1.call-start = ((), (), s32[]{:S(2)}) async-start(), calls=%async_computation.1 | async-start | bytes 6291456 | tf_op jit(solution)/shard_map/all_gather | solution.py:74
  6.5 30.3 %collective-permute-start = (bf16[600,1024]{1,0:T(8,128)(2,1)}, bf16[600,1024]{1,0:T(8,128)(2,1)}, u32[]{:S(2)}, u32[]{:S(2)}) collective-permute-start(bf16[600,1024]{1,0:T(8,128)(2,1)} %param.11), channel_id=1, source_target_pairs={{0,2},{2,0},{4,6},{6,4},{8,10},{10,8},{12,14},{14,12},{1,3},{3,1},... | collective-permute-start | bytes 3686408 | tf_op jit(solution)/shard_map/ppermute | solution.py:80
  40.3 54.7 %collective-permute-start.1 = (bf16[600,2048]{1,0:T(8,128)(2,1)S(1)}, bf16[600,2048]{1,0:T(8,128)(2,1)}, u32[]{:S(2)}, u32[]{:S(2)}) collective-permute-start(bf16[600,2048]{1,0:T(8,128)(2,1)S(1)} %maximum_select_fusion.2), channel_id=1, source_target_pairs={{0,4},{2,6},{4,0},{6,2},{8,12},{10,14},{12,8},{14,10},{1,5},{3,7},... | collective-permute-start | bytes 7372808 | tf_op jit(solution)/shard_map/ppermute | solution.py:80
  101.7 212.9 %collective-permute-start.2 = (bf16[600,4096]{1,0:T(8,128)(2,1)}, bf16[600,4096]{1,0:T(8,128)(2,1)}, u32[]{:S(2)}, u32[]{:S(2)}) collective-permute-start(bf16[600,4096]{1,0:T(8,128)(2,1)} %maximum_select_fusion.1), channel_id=1, source_target_pairs={{0,8},{2,10},{4,12},{6,14},{8,0},{10,2},{12,4},{14,6},{1,9},{3,11}... | collective-permute-start | bytes 14745608 | tf_op jit(solution)/shard_map/ppermute | solution.py:80
  104.3 320.0 %all-gather.7.cloned.1.call-start = ((), (), s32[]{:S(2)}) async-start(), calls=%async_computation.2 | async-start | bytes 2764800 | tf_op jit(solution)/shard_map/all_gather | solution.py:93
  104.4 222.1 %copy-start.5 = (f32[8192]{0:T(1024)S(1)}, f32[8192]{0:T(1024)}, u32[]{:S(2)}) copy-start(f32[8192]{0:T(1024)} %param.12) | copy-start | bytes 98308
  326.4 11.7 %copy-start.1 = (s32[64,16]{0,1:T(8,128)S(1)}, s32[64,16]{0,1:T(8,128)}, u32[]{:S(2)}) copy-start(s32[64,16]{0,1:T(8,128)} %param.14) | copy-start | bytes 12292
  338.1 93.2 %all-gather.9.cloned.1.call-start = ((), (), s32[]{:S(2)}) async-start(), calls=%async_computation.3 | async-start | bytes 25165824 | tf_op jit(solution)/shard_map/all_gather | solution.py:72
  377.7 0.7 copy-start.2
  377.7 94.8 %all-gather.11.cloned.1.call-start = ((), (), s32[]{:S(2)}) async-start(), calls=%async_computation.4 | async-start | bytes 25165824 | tf_op jit(solution)/shard_map/all_gather | solution.py:75
  421.7 0.7 copy-start.3
  421.7 1.0 copy-start.4
  421.7 394.4 %reduce-scatter.2.cloned.1.call-start = ((), (), s32[]{:S(2)}) async-start(), calls=%async_computation.5 | async-start | bytes 22118400 | tf_op jit(solution)/shard_map/reduce_scatter | solution.py:129
  462.5 5.5 copy-start
Sparse Core Ops, SparseCore 0:
  104.5 12.8 all-gather.4
  338.2 56.4 all-gather.6
  396.3 28.2 all-gather.8
  426.0 31.2 all-gather.10
  490.5 325.5 reduce-scatter.1
